TPU v7x, 32 devices: a whole 2x2x4 slice. The times are simulated.
32 devices in a mesh: ctx: 8 (over y, x, core), tp: 4 (over z).
Axes of the slice: x: 2, y: 2, z: 4, core: 2. Of those that a mesh axis runs over, the one named last changes fastest.
Arguments:
- tokens: bfloat16 [4096, 4096], P(('ctx', 'tp')), may hold values from -6 to 6
- spike_query: int32 [4096, 32], P('ctx', 'tp'), may hold values 0 or 1
- spike_key: int32 [4096, 32], P('ctx', 'tp'), may hold values 0 or 1
- qkv_weight: bfloat16 [4096, 3, 4096], P(None, None, 'tp'), may hold values from -0.09375 to 0.09375
- qkv_blocks: int32 [3, 32, 32], P(None, None, 'tp'), may hold values 0 or 1
- out_weight: bfloat16 [4096, 4096], P('tp'), may hold values from -0.09375 to 0.09375
- out_blocks: int32 [32, 32], P('tp'), may hold values 0 or 1
- cotangent: bfloat16 [4096, 4096], P(('ctx', 'tp')), may hold values from -6 to 6
Outputs:
- layer_out: bfloat16 [4096, 4096], P(('ctx', 'tp'))
- token_grad: bfloat16 [4096, 4096], P(('ctx', 'tp'))
- qkv_grad: float32 [4096, 3, 4096], P('ctx', None, 'tp')
- out_grad: float32 [4096, 4096], P('tp', 'ctx')
All inputs are finite; a program needn't handle non-finite values. No bound on the sum of `spike_query` or of `spike_key` or of `qkv_blocks` or of `out_blocks` on one device may be relied on, other than what follows from the above.
Results may differ from a plain program's by a relative error of at most 0.014.
Values may be sent and summed in bfloat16 or wider, within the bound.
No kernel may reach another device: no remote copies, remote signals or barrier semaphores. Data moves between devices by JAX's collectives and lax.ppermute only.
A program may use at most 320 MiB of HBM per device.

v0:
```python
import math
import jax
import jax.numpy as jnp
from jax import lax
from jax.sharding import PartitionSpec as P

BLOCK = 128
EPSILON = 1e-05


def carried_in(value, axis, join, neutral):
    place = lax.axis_index(axis)
    gathered = lax.all_gather(value.astype(jnp.bfloat16), axis)
    state = jnp.zeros_like(value) + jnp.asarray(neutral, value.dtype)

    def carried_one(lap, state):
        return join(state, lax.dynamic_index_in_dim(gathered, lap, 0, False).astype(value.dtype))

    return lax.fori_loop(0, place, carried_one, state)


def entering(value, axis, join, neutral):
    count = lax.axis_size(axis)
    place = lax.axis_index(axis)
    ahead = count - 1 - place
    gathered = lax.all_gather(
        value.astype(jnp.bfloat16 if value.dtype == jnp.float32 else value.dtype), axis
    )
    state = jnp.zeros_like(value) + jnp.asarray(neutral, value.dtype)

    def entering_one(lap, state):
        source = count - 1 - lap
        return join(state, lax.dynamic_index_in_dim(gathered, source, 0, False).astype(value.dtype))

    return lax.fori_loop(0, ahead, entering_one, state)


def expand_blocks(blocks):
    row_blocks, col_blocks = blocks.shape
    spread = jnp.broadcast_to(
        blocks.astype(jnp.bfloat16)[:, None, :, None], (row_blocks, BLOCK, col_blocks, BLOCK)
    )
    return spread.reshape(row_blocks * BLOCK, col_blocks * BLOCK)


def qkv_keep_table(qkv_blocks):
    tables = [expand_blocks(qkv_blocks[projection]) for projection in range(3)]
    return jnp.stack(tables, axis=1)


def add_states(earlier, following):
    return earlier + following


def on_device(
    tokens, spike_query, spike_key, qkv_weight, qkv_blocks, out_weight, out_blocks, cotangent
):
    model_width = tokens.shape[1]
    block_rows = spike_query.shape[0]
    local_heads = spike_query.shape[1]
    features = qkv_weight.shape[2]
    head_width = features // local_heads
    row_blocks = model_width // BLOCK
    col_blocks = features // BLOCK
    highest = lax.Precision.HIGHEST
    qkv_mask = jnp.transpose(qkv_blocks, (1, 0, 2)).astype(jnp.bfloat16)
    qkv_used = (
        qkv_weight.reshape(row_blocks, BLOCK, 3, col_blocks, BLOCK) * qkv_mask[:, None, :, :, None]
    ).reshape(model_width, 3 * features)
    out_used = (
        out_weight.reshape(col_blocks, BLOCK, row_blocks, BLOCK)
        * out_blocks.astype(jnp.bfloat16)[:, None, :, None]
    ).reshape(features, model_width)
    gathered = lax.all_gather(tokens, "tp", axis=0, tiled=True)
    projected = jnp.dot(gathered, qkv_used, preferred_element_type=jnp.float32).astype(jnp.bfloat16)
    projected = projected.reshape(block_rows, 3, local_heads, head_width)
    query_spikes = spike_query.astype(jnp.bfloat16)[:, :, None]
    key_spikes = spike_key.astype(jnp.bfloat16)[:, :, None]
    query_spiked = projected[:, 0] * query_spikes
    key_spiked = projected[:, 1] * key_spikes
    values = projected[:, 2]
    query_wide = query_spiked.astype(jnp.float32)
    key_wide = key_spiked.astype(jnp.float32)
    local_state = jnp.einsum("shd,she->hde", key_spiked, values, preferred_element_type=jnp.float32)
    zeros_state = jnp.zeros_like(local_state)
    prior_state = carried_in(local_state, "ctx", add_states, zeros_state)
    positions = lax.iota(jnp.int32, block_rows)
    causal_keep = positions[:, None] >= positions[None, :]
    scores = jnp.einsum(
        "thd,shd->hts", query_spiked, key_spiked, preferred_element_type=jnp.float32
    )
    scores = jnp.where(causal_keep, scores, 0.0).astype(jnp.bfloat16)
    mixed_rows = jnp.einsum("hts,she->the", scores, values, preferred_element_type=jnp.float32)
    mixed_rows = mixed_rows + jnp.einsum("thd,hde->the", query_wide, prior_state, precision=highest)
    inv_rms = lax.rsqrt(jnp.mean(mixed_rows * mixed_rows, axis=-1, keepdims=True) + EPSILON)
    normed = mixed_rows * inv_rms
    attended = normed.astype(jnp.bfloat16).reshape(block_rows, features)
    head_sum = lax.psum_scatter(
        jnp.dot(attended, out_used, preferred_element_type=jnp.float32).astype(jnp.bfloat16),
        "tp",
        scatter_dimension=0,
        tiled=True,
    ).astype(jnp.float32)
    layer_out = (tokens.astype(jnp.float32) + head_sum).astype(jnp.bfloat16)
    grad_rows = lax.all_gather(cotangent, "tp", axis=0, tiled=True)
    ctx_count = lax.axis_size("ctx")
    ctx_place = lax.axis_index("ctx")
    slice_rows = model_width // ctx_count
    slice_blocks = slice_rows // BLOCK
    norm_factor = 1.0 / math.sqrt(block_rows * ctx_count)
    out_part = jnp.einsum("tm,tf->mf", grad_rows, attended, preferred_element_type=jnp.float32)
    out_sum = lax.psum_scatter(
        out_part.astype(jnp.bfloat16), "ctx", scatter_dimension=0, tiled=True
    ).astype(jnp.float32)
    out_keep = lax.dynamic_slice_in_dim(out_blocks, ctx_place * slice_blocks, slice_blocks, 1)
    out_keep = jnp.broadcast_to(
        jnp.transpose(out_keep).astype(jnp.float32)[:, None, :, None],
        (slice_blocks, BLOCK, col_blocks, BLOCK),
    ).reshape(slice_rows, features)
    out_grad = jnp.transpose(out_sum * out_keep * norm_factor)
    grad_attended = jnp.einsum("tm,fm->tf", grad_rows, out_used, preferred_element_type=jnp.float32)
    grad_attended = grad_attended.reshape(block_rows, local_heads, head_width)
    inner_mean = jnp.mean(grad_attended * normed, axis=-1, keepdims=True)
    grad_mixed = inv_rms * (grad_attended - normed * inner_mean)
    grad_low = grad_mixed.astype(jnp.bfloat16)
    local_adjoint = jnp.einsum("thd,the->hde", query_wide, grad_mixed, precision=highest)
    after_state = entering(local_adjoint, "ctx", add_states, zeros_state)
    adjoint_scores = jnp.einsum(
        "the,she->hts", grad_low, values, preferred_element_type=jnp.float32
    )
    adjoint_scores = jnp.where(causal_keep, adjoint_scores, 0.0).astype(jnp.bfloat16)
    grad_query = jnp.einsum(
        "hts,shd->thd", adjoint_scores, key_spiked, preferred_element_type=jnp.float32
    )
    grad_query = grad_query + jnp.einsum("the,hde->thd", grad_mixed, prior_state, precision=highest)
    grad_key = jnp.einsum(
        "hts,thd->shd", adjoint_scores, query_spiked, preferred_element_type=jnp.float32
    )
    grad_key = grad_key + jnp.einsum(
        "she,hde->shd", values.astype(jnp.float32), after_state, precision=highest
    )
    grad_value = jnp.einsum("hts,the->she", scores, grad_low, preferred_element_type=jnp.float32)
    grad_value = grad_value + jnp.einsum("shd,hde->she", key_wide, after_state, precision=highest)
    grad_proj = jnp.stack(
        [
            (grad_query * query_spikes.astype(jnp.float32)).astype(jnp.bfloat16),
            (grad_key * key_spikes.astype(jnp.float32)).astype(jnp.bfloat16),
            grad_value.astype(jnp.bfloat16),
        ],
        axis=1,
    ).reshape(block_rows, 3 * features)
    qkv_part = jnp.einsum("tm,tc->mc", gathered, grad_proj, preferred_element_type=jnp.float32)
    qkv_sum = lax.psum_scatter(
        qkv_part.astype(jnp.bfloat16), "ctx", scatter_dimension=0, tiled=True
    ).astype(jnp.float32)
    qkv_keep = lax.dynamic_slice_in_dim(qkv_mask, ctx_place * slice_blocks, slice_blocks, 0)
    qkv_keep = jnp.broadcast_to(
        qkv_keep.astype(jnp.float32)[:, None, :, :, None],
        (slice_blocks, BLOCK, 3, col_blocks, BLOCK),
    ).reshape(slice_rows, 3, features)
    qkv_grad = qkv_sum.reshape(slice_rows, 3, features) * qkv_keep * norm_factor
    token_sum = lax.psum_scatter(
        jnp.einsum("tc,mc->tm", grad_proj, qkv_used, preferred_element_type=jnp.float32).astype(
            jnp.bfloat16
        ),
        "tp",
        scatter_dimension=0,
        tiled=True,
    ).astype(jnp.float32)
    token_grad = (cotangent.astype(jnp.float32) + token_sum).astype(jnp.bfloat16)
    return (layer_out, token_grad, qkv_grad, out_grad)


def solution(mesh):
    placed = (
        P(("ctx", "tp"), None),
        P("ctx", "tp"),
        P("ctx", "tp"),
        P(None, None, "tp"),
        P(None, None, "tp"),
        P("tp", None),
        P("tp", None),
        P(("ctx", "tp"), None),
    )
    return jax.shard_map(
        on_device,
        mesh=mesh,
        in_specs=placed,
        out_specs=(
            P(("ctx", "tp"), None),
            P(("ctx", "tp"), None),
            P("ctx", None, "tp"),
            P("tp", "ctx"),
        ),
        check_vma=False,
    )
```

profile of v0, /device:TPU:0, one launch (start us, length us, event | category | flops | bytes accessed | tf_op | source)
XLA Modules:
  0.0 764.5 jit_solution(3684629579513583311)
XLA Ops:
  8.8 8.7 %mul.111 = bf16[32,128,3,8,128]{4,3,2,1,0:T(8,128)(2,1)} broadcast(bf16[32,3,8]{2,1,0:T(4,128)(2,1)S(1)} %copy.47), dimensions={0,2,3} | broadcast | bytes 25167360 | tf_op jit(solution)/shard_map/mul | solution.py:68
  17.5 37.4 %mul.112 = bf16[4096,3072]{1,0:T(8,128)(2,1)} reshape(bf16[32,128,3,8,128]{4,3,2,1,0:T(8,128)(2,1)} %mul.111) | data formatting | bytes 50331648 | tf_op jit(solution)/shard_map/mul | solution.py:68
  54.9 31.5 %copy.48 = bf16[4096,3072]{0,1:T(8,128)(2,1)} copy(bf16[4096,3072]{1,0:T(8,128)(2,1)} %mul.112) | data formatting | bytes 50331648 | tf_op jit(solution)/shard_map/mul | solution.py:68
  86.4 33.6 %copy.46 = bf16[4096,3,1024]{0,2,1:T(8,128)(2,1)} copy(bf16[4096,3,1024]{2,0,1:T(8,128)(2,1)} %param.15) | data formatting | bytes 50331648 | tf_op args[3]
  120.0 25.4 %bitcast_multiply_fusion = bf16[4096,3072]{0,1:T(8,128)(2,1)} fusion(bf16[4096,3072]{0,1:T(8,128)(2,1)} %copy.48, bf16[4096,3,1024]{0,2,1:T(8,128)(2,1)} %copy.46), kind=kLoop, calls=%fused_computation.2 | loop fusion | flops 12582912 | bytes 75497472 | tf_op jit(solution)/shard_map/mul | solution.py:68
  145.4 18.2 %convolution_convert_fusion.2 = bf16[3072,512]{1,0:T(8,128)(2,1)S(1)} fusion(bf16[4096,3072]{0,1:T(8,128)(2,1)} %bitcast_multiply_fusion, bf16[512,4096]{1,0:T(8,128)(2,1)} %all-gather.7.cloned.1.call-done), kind=kOutput, calls=%fused_computation.11 | convolution fusion | flops 12886474752 | bytes 32505856 | tf_op jit(solution)/shard_map/dot_general | solution.py:75
  172.3 23.8 %all-gather.11.cloned.1.call-done = bf16[64,128,128]{2,1,0:T(8,128)(2,1)} async-done(((bf16[8,128,128]{2,1,0:T(8,128)(2,1)}), bf16[64,128,128]{2,1,0:T(8,128)(2,1)}) %all-gather.11.cloned.1.call-update) | async-done | bytes 2097168 | tf_op jit(solution)/shard_map/all_gather | solution.py:13
  199.8 78.7 %all-gather.9.cloned.1.call-done = bf16[512,4096]{1,0:T(8,128)(2,1)} async-done(((bf16[128,4096]{1,0:T(8,128)(2,1)}), bf16[512,4096]{1,0:T(8,128)(2,1)}) %all-gather.9.cloned.1.call-update) | async-done | bytes 4194320 | tf_op jit(solution)/shard_map/all_gather | solution.py:105
  279.6 12.4 %multiply_reduce_fusion = (f32[512,8]{0,1:T(8,128)S(1)}, f32[1024,512]{1,0:T(8,128)S(1)}) fusion(f32[8,128,512]{2,1,0:T(8,128)S(1)} %get-tuple-element.108, f32[512,8]{0,1:T(8,128)S(1)} %add_rsqrt_fusion, bf16[512,4096]{1,0:T(8,128)(2,1)} %all-gather.9.cloned.1.call-done, bf16[1024,4096]{1,0:T(8,128)(2,1)} %param.17, bf16[128,8,32,128]{3,2,1,0:T(8,128)(2,1)S(1)} %bitcast.142), kind=kOutput, calls=%fused_computation.27 | convolution fusion | flops 4300730368 | bytes 25198592 | tf_op jit(solution)/shard_map/tm,fm->tf/dot_general | solution.py:121
  298.6 13.4 %convolution_convert_fusion.1 = bf16[512,4096]{1,0:T(8,128)(2,1)} fusion(bf16[512,1024]{0,1:T(8,128)(2,1)} %bitcast.159, bf16[1024,4096]{1,0:T(8,128)(2,1)} %param.17, bf16[128,8,32,128]{3,2,1,0:T(8,128)(2,1)} %bitcast.143), kind=kOutput, calls=%fused_computation.10 | convolution fusion | flops 4301258752 | bytes 22020096 | tf_op jit(solution)/shard_map/dot_general | solution.py:99
  312.1 8.8 %mul.111.clone = bf16[32,128,3,8,128]{1,0,4,3,2:T(8,128)(2,1)} broadcast(bf16[32,3,8]{0,2,1:T(8,128)(2,1)S(1)} %convert_bitcast_fusion.4), dimensions={0,2,3} | broadcast | bytes 25167360 | tf_op jit(solution)/shard_map/mul | solution.py:68
  320.9 37.5 %mul.132 = bf16[4096,3,1024]{0,2,1:T(8,128)(2,1)} reshape(bf16[32,128,3,8,128]{1,0,4,3,2:T(8,128)(2,1)} %mul.111.clone) | data formatting | bytes 50331648 | tf_op jit(solution)/shard_map/mul | solution.py:68
  358.4 28.7 %mul.133 = bf16[4096,3,1024]{0,2,1:T(8,128)(2,1)} multiply(bf16[4096,3,1024]{0,2,1:T(8,128)(2,1)} %copy.46, bf16[4096,3,1024]{0,2,1:T(8,128)(2,1)} %mul.132) | non-fusion elementwise | flops 12582912 | bytes 75497472 | tf_op jit(solution)/shard_map/mul | solution.py:68
  399.3 7.9 %while.23 = (s32[]{:T(128)}, f32[8,128,128]{2,1,0:T(8,128)S(1)}, s32[]{:T(128)}, bf16[8,8,128,128]{3,2,1,0:T(8,128)(2,1)}, s32[]{:T(128)}, /*index=5*/s32[]{:T(128)}, s32[]{:T(128)}, s32[]{:T(128)}) while((s32[]{:T(128)}, f32[8,128,128]{2,1,0:T(8,128)S(1)}, s32[]{:T(128)}, bf16[8,8,128,128]{3,2,1,0:T(8,128)(2,1)}, s32[]{:T(128)}, ...), condition=%wide.region_6.7_spmd, body=%wide.region_5.6_spmd.sunk | while | flops 262150 | bytes 1310863 | solution.py:35
  413.1 19.5 %convolution_convert_fusion = bf16[512,4096]{1,0:T(8,128)(2,1)} fusion(bf16[512,3072]{0,1:T(8,128)(2,1)S(1)} %bitcast.156, bf16[4096,3072]{0,1:T(8,128)(2,1)} %bitcast.144), kind=kOutput, calls=%fused_computation.9 | convolution fusion | flops 12886999040 | bytes 32505856 | tf_op jit(solution)/shard_map/tc,mc->tm/dot_general | solution.py:163
  432.9 10.5 %convert_bitcast_fusion.1 = bf16[4096,1024]{0,1:T(8,128)(2,1)} fusion(bf16[512,1024]{0,1:T(8,128)(2,1)} %bitcast.160, bf16[512,4096]{1,0:T(8,128)(2,1)} %all-gather.9.cloned.1.call-done), kind=kOutput, calls=%fused_computation.5 | convolution fusion | flops 4299161600 | bytes 13631488 | tf_op jit(solution)/shard_map/tm,tf->mf/dot_general | solution.py:111
  443.4 19.1 %convert_bitcast_fusion = bf16[4096,3072]{0,1:T(8,128)(2,1)} fusion(bf16[512,3072]{0,1:T(8,128)(2,1)S(1)} %bitcast.157, bf16[512,4096]{1,0:T(8,128)(2,1)} %all-gather.7.cloned.1.call-done), kind=kOutput, calls=%fused_computation.3 | convolution fusion | flops 12897484800 | bytes 32505856 | tf_op jit(solution)/shard_map/tm,tc->mc/dot_general | solution.py:152
  463.5 3.2 broadcast_in_dim.38
  466.7 7.2 reshape.76
  476.4 29.7 %reduce-scatter.7.cloned.1.call-done = bf16[128,4096]{1,0:T(8,128)(2,1)} async-done(((bf16[512,4096]{1,0:T(8,128)(2,1)}), bf16[128,4096]{1,0:T(8,128)(2,1)}) %reduce-scatter.7.cloned.1.call-update) | async-done | bytes 1048592 | tf_op jit(solution)/shard_map/reduce_scatter | solution.py:162
  508.5 72.8 %reduce-scatter.11.cloned.1.call-done = bf16[512,1024]{0,1:T(8,128)(2,1)} async-done(((bf16[4096,1024]{0,1:T(8,128)(2,1)}), bf16[512,1024]{0,1:T(8,128)(2,1)}) %reduce-scatter.11.cloned.1.call-update) | async-done | bytes 1048592 | tf_op jit(solution)/shard_map/reduce_scatter | solution.py:112
  584.6 157.7 %reduce-scatter.9.cloned.1.call-done = bf16[512,3072]{0,1:T(8,128)(2,1)} async-done(((bf16[4096,3072]{0,1:T(8,128)(2,1)}), bf16[512,3072]{0,1:T(8,128)(2,1)}) %reduce-scatter.9.cloned.1.call-update) | async-done | bytes 3145744 | tf_op jit(solution)/shard_map/reduce_scatter | solution.py:153
  742.3 5.4 copy.64
  747.7 9.5 %multiply_multiply_fusion = f32[512,3,1024]{2,0,1:T(8,128)} fusion(f32[512,3,1024]{2,0,1:T(8,128)} %copy.64, f32[512,3,1024]{2,0,1:T(8,128)} %reshape.76), kind=kLoop, calls=%fused_computation.8 | loop fusion | flops 3145728 | bytes 18874368 | tf_op jit(solution)/shard_map/mul | solution.py:161
  (89 shorter events, 56.6 us)
Async XLA Ops:
  7.2 138.3 %all-gather.7.cloned.1.call-start = ((), (), s32[]{:S(2)}) async-start(), calls=%async_computation.4 | async-start | bytes 5242880 | tf_op jit(solution)/shard_map/all_gather | solution.py:74
  7.9 188.2 %all-gather.11.cloned.1.call-start = ((), (), s32[]{:S(2)}) async-start(), calls=%async_computation.10 | async-start | bytes 2359296 | tf_op jit(solution)/shard_map/all_gather | solution.py:13
  86.4 33.6 %copy-start.11 = (s32[512,8]{0,1:T(8,128)S(1)}, s32[512,8]{0,1:T(8,128)}, u32[]{:S(2)}) copy-start(s32[512,8]{0,1:T(8,128)} %param.13) | copy-start | bytes 49156
  86.4 33.6 %copy-start.12 = (s32[512,8]{0,1:T(8,128)S(1)}, s32[512,8]{0,1:T(8,128)}, u32[]{:S(2)}) copy-start(s32[512,8]{0,1:T(8,128)} %param.14) | copy-start | bytes 49156
  163.6 3.9 copy-start.1
  163.6 2.3 copy-start.13
  165.2 113.3 %all-gather.9.cloned.1.call-start = ((), (), s32[]{:S(2)}) async-start(), calls=%async_computation.6 | async-start | bytes 5242880 | tf_op jit(solution)/shard_map/all_gather | solution.py:105
  165.9 233.3 %all-gather.13.cloned.1.call-start = ((), (), s32[]{:S(2)}) async-start(), calls=%async_computation.11 | async-start | bytes 2359296 | tf_op jit(solution)/shard_map/all_gather | solution.py:26
  167.5 2.0 copy-start.4
  199.7 79.9 %copy-start.3 = (f32[8,128,512]{2,1,0:T(8,128)}, f32[8,128,512]{2,1,0:T(8,128)S(1)}, u32[]{:S(2)}) copy-start(f32[8,128,512]{2,1,0:T(8,128)S(1)} %get-tuple-element.108) | copy-start | bytes 6291460
  279.6 12.4 %copy-start = (bf16[8,128,32,128]{3,2,1,0:T(8,128)(2,1)}, bf16[8,128,32,128]{3,2,1,0:T(8,128)(2,1)S(1)}, u32[]{:S(2)}) copy-start(bf16[8,128,32,128]{3,2,1,0:T(8,128)(2,1)S(1)} %mul.121) | copy-start | bytes 25165828
  298.4 175.5 %reduce-scatter.5.cloned.1.call-start = ((), (), s32[]{:S(2)}) async-start(), calls=%async_computation.5 | async-start | bytes 5242880 | tf_op jit(solution)/shard_map/reduce_scatter | solution.py:98
  312.0 194.0 %reduce-scatter.7.cloned.1.call-start = ((), (), s32[]{:S(2)}) async-start(), calls=%async_computation.7 | async-start | bytes 5242880 | tf_op jit(solution)/shard_map/reduce_scatter | solution.py:162
  387.1 2.7 copy-start.2
  394.2 2.9 copy-start.5
  407.1 3.2 copy-start.6
  410.3 2.5 copy-start.9
  432.6 148.7 %reduce-scatter.11.cloned.1.call-start = ((), (), s32[]{:S(2)}) async-start(), calls=%async_computation.9 | async-start | bytes 9437184 | tf_op jit(solution)/shard_map/reduce_scatter | solution.py:112
  443.4 298.9 %reduce-scatter.9.cloned.1.call-start = ((), (), s32[]{:S(2)}) async-start(), calls=%async_computation.8 | async-start | bytes 28311552 | tf_op jit(solution)/shard_map/reduce_scatter | solution.py:153
  462.6 0.7 copy-start.10
  466.7 7.2 copy-start.14
  466.7 7.2 copy-start.7
  473.8 32.3 %copy-start.8 = (bf16[128,4096]{1,0:T(8,128)(2,1)S(1)}, bf16[128,4096]{1,0:T(8,128)(2,1)}, u32[]{:S(2)}) copy-start(bf16[128,4096]{1,0:T(8,128)(2,1)} %param.19) | copy-start | bytes 3145732
Sparse Core Ops, SparseCore 0:
  9.6 83.4 all-gather.6
  165.3 30.7 all-gather.10
  197.6 80.7 all-gather.8
  298.5 26.4 all-gather.12
  327.1 76.8 reduce-scatter.4
  432.7 73.3 reduce-scatter.6
  509.5 71.7 reduce-scatter.10
  585.4 156.8 reduce-scatter.8
where the time goes:
time: 775 us; the launch traced here: 765 us
  waiting for transfers between devices  364 us (47%)
  local copies, waits for them, and re-layouts  179 us (23%)
  matrix products  122 us (16%)
  other arithmetic  83.5 us (11%)
  between operations  14.9 us (2%)
    reduce_scatter x1, waiting for transfers between devices, on_device(): lax.psum_scatter(qkv_part.astype(jnp.bfloat16), 'ctx', scatter_dimension=...  158 us
    mul x5, local copies, waits for them, and re-layouts, on_device(): qkv_weight.reshape(row_blocks, BLOCK, 3, col_blocks, BLOCK)  124 us
    all_gather x1, waiting for transfers between devices, on_device(): grad_rows = lax.all_gather(cotangent, 'tp', axis=0, tiled=True)  78.7 us
    reduce_scatter x1, waiting for transfers between devices, on_device(): lax.psum_scatter(out_part.astype(jnp.bfloat16), 'ctx', scatter_dimension=...  72.8 us
    mul x2, other arithmetic, on_device(): qkv_weight.reshape(row_blocks, BLOCK, 3, col_blocks, BLOCK)  54.1 us
    unnamed x31, local copies, waits for them, and re-layouts  37.1 us
    reduce_scatter x1, waiting for transfers between devices, on_device(): lax.psum_scatter(jnp.einsum('tc,mc->tm', grad_proj, qkv_used, preferred_e...  29.7 us
    all_gather x1, waiting for transfers between devices, carried_in(): gathered = lax.all_gather(value.astype(jnp.bfloat16), axis)  23.8 us
  transfers between devices with their start and end apart: 8, of which 5 were waited for; matrix products, arithmetic and copies ran while one was open for 43% of the time, Pallas kernels for 0%

commit v1 on v0

--- a/solution.py
+++ b/solution.py
@@ -3,9 +3,17 @@
 import jax.numpy as jnp
 from jax import lax
 from jax.sharding import PartitionSpec as P
+from jax.lax import axis_index, axis_size, ppermute
 
 BLOCK = 128
 EPSILON = 1e-05
+
+
+def measure_sections(t0, d_out):
+    part_now = list(t0.shape[1:])
+    part_now[d_out] *= t0.shape[0]
+    big = jnp.moveaxis(t0, 0, d_out).reshape(part_now)
+    return big
 
 
 def carried_in(value, axis, join, neutral):
@@ -102,7 +110,27 @@
         tiled=True,
     ).astype(jnp.float32)
     layer_out = (tokens.astype(jnp.float32) + head_sum).astype(jnp.bfloat16)
-    grad_rows = lax.all_gather(cotangent, "tp", axis=0, tiled=True)
+    n_slots = axis_size("tp")
+    rows = []
+    c = 0
+    while c < n_slots:
+        rows.append((c, (c + 1) % n_slots))
+        c += 1
+    pool = []
+    for src_i, i0 in rows:
+        pool.append((i0, src_i))
+    clean, heard = ([], [])
+    idx = 0
+    while idx < n_slots - 1:
+        if idx % 2 == 0:
+            clean.append(ppermute(clean[-1] if clean else cotangent, axis_name="tp", perm=rows))
+        else:
+            heard.append(ppermute(heard[-1] if heard else cotangent, axis_name="tp", perm=pool))
+        idx += 1
+    field_out = jnp.stack([*clean[::-1], cotangent, *heard], axis=0)
+    raw_out = axis_index("tp") - len(clean)
+    field_out = field_out[(jnp.arange(n_slots) - raw_out) % n_slots]
+    grad_rows = measure_sections(field_out, 0)
     ctx_count = lax.axis_size("ctx")
     ctx_place = lax.axis_index("ctx")
     slice_rows = model_width // ctx_count

time: 775 us -> 726 us (0.937)
  waiting for transfers between devices: 364 us -> 300 us
  other arithmetic: 83.5 us -> 93.5 us
  matrix products: 122 us -> 113 us
    all_gather x1 -> x0, waiting for transfers between devices: 78.7 us -> none  [on_device(): grad_rows = lax.all_gather(cotangent, 'tp', axis=0, tiled=True)]
    ppermute x0 -> x3, waiting for transfers between devices: none -> 36.9 us  [the longest x2 23.3 us: on_device(): ppermute(clean[-1] if clean else cotangent, axis_name='tp', perm=rows)]
    all_gather x1, waiting for transfers between devices: 23.8 us -> 0.01 us  [carried_in(): gathered = lax.all_gather(value.astype(jnp.bfloat16), axis)]
    mul x0 -> x1, other arithmetic: none -> 8.95 us  [on_device(): out_weight.reshape(col_blocks, BLOCK, row_blocks, BLOCK)]
    unnamed x31 -> x32, local copies, waits for them, and re-layouts: 37.1 us -> 38.9 us
  transfers between devices with their start and end apart: 8 -> 10, of which waited for: 5 -> 5; matrix products, arithmetic and copies ran while one was open for 43% -> 50% of each run, Pallas kernels for 0% -> 0%
where the time goes in v1:
time: 726 us; the launch traced here: 714 us
  waiting for transfers between devices  300 us (41%)
  local copies, waits for them, and re-layouts  186 us (26%)
  matrix products  113 us (16%)
  other arithmetic  93.5 us (13%)
  between operations  14.6 us (2%)
    reduce_scatter x1, waiting for transfers between devices, on_device(): lax.psum_scatter(qkv_part.astype(jnp.bfloat16), 'ctx', scatter_dimension=...  157 us
    mul x5, local copies, waits for them, and re-layouts, on_device(): qkv_weight.reshape(row_blocks, BLOCK, 3, col_blocks, BLOCK)  124 us
    reduce_scatter x1, waiting for transfers between devices, on_device(): lax.psum_scatter(out_part.astype(jnp.bfloat16), 'ctx', scatter_dimension=...  72.7 us
    mul x2, other arithmetic, on_device(): qkv_weight.reshape(row_blocks, BLOCK, 3, col_blocks, BLOCK)  54.3 us
    unnamed x32, local copies, waits for them, and re-layouts  38.9 us
    reduce_scatter x1, waiting for transfers between devices, on_device(): lax.psum_scatter(jnp.einsum('tc,mc->tm', grad_proj, qkv_used, preferred_e...  32.6 us
    ppermute x2, waiting for transfers between devices, on_device(): ppermute(clean[-1] if clean else cotangent, axis_name='tp', perm=rows)  23.3 us
    dot_general x1, matrix products, on_device(): jnp.einsum('tc,mc->tm', grad_proj, qkv_used, preferred_element_type=jnp.f...  19.6 us
  transfers between devices with their start and end apart: 10, of which 5 were waited for; matrix products, arithmetic and copies ran while one was open for 50% of the time, Pallas kernels for 0%

profile of v1, /device:TPU:0, one launch (start us, length us, event | category | flops | bytes accessed | tf_op | source)
XLA Modules:
  0.0 713.6 jit_solution(16860453401116775030)
XLA Ops:
  11.8 8.9 %mul.111 = bf16[32,128,3,8,128]{4,3,2,1,0:T(8,128)(2,1)} broadcast(bf16[32,3,8]{2,1,0:T(4,128)(2,1)S(1)} %copy.51), dimensions={0,2,3} | broadcast | bytes 25167360 | tf_op jit(solution)/shard_map/mul | solution.py:76
  20.7 37.3 %mul.112 = bf16[4096,3072]{1,0:T(8,128)(2,1)} reshape(bf16[32,128,3,8,128]{4,3,2,1,0:T(8,128)(2,1)} %mul.111) | data formatting | bytes 50331648 | tf_op jit(solution)/shard_map/mul | solution.py:76
  58.0 31.6 %copy.52 = bf16[4096,3072]{0,1:T(8,128)(2,1)} copy(bf16[4096,3072]{1,0:T(8,128)(2,1)} %mul.112) | data formatting | bytes 50331648 | tf_op jit(solution)/shard_map/mul | solution.py:76
  89.6 33.6 %copy.50 = bf16[4096,3,1024]{0,2,1:T(8,128)(2,1)} copy(bf16[4096,3,1024]{2,0,1:T(8,128)(2,1)} %param.15) | data formatting | bytes 50331648 | tf_op args[3]
  123.2 25.4 %bitcast_multiply_fusion = bf16[4096,3072]{0,1:T(8,128)(2,1)} fusion(bf16[4096,3072]{0,1:T(8,128)(2,1)} %copy.52, bf16[4096,3,1024]{0,2,1:T(8,128)(2,1)} %copy.50), kind=kLoop, calls=%fused_computation.3 | loop fusion | flops 12582912 | bytes 75497472 | tf_op jit(solution)/shard_map/mul | solution.py:76
  148.7 18.2 %convolution_convert_fusion.3 = bf16[3072,512]{1,0:T(8,128)(2,1)S(1)} fusion(bf16[4096,3072]{0,1:T(8,128)(2,1)} %bitcast_multiply_fusion, bf16[512,4096]{1,0:T(8,128)(2,1)} %all-gather.6.cloned.1.call-done), kind=kOutput, calls=%fused_computation.12 | convolution fusion | flops 12886474752 | bytes 32505856 | tf_op jit(solution)/shard_map/dot_general | solution.py:83
  172.0 9.0 %bitcast_multiply_fusion.1 = bf16[1024,4096]{1,0:T(8,128)(2,1)} fusion(bf16[1024,4096]{1,0:T(8,128)(2,1)} %param.17, bf16[128,8,32,128]{3,2,1,0:T(8,128)(2,1)S(1)} %bitcast.141), kind=kLoop, calls=%fused_computation.5 | loop fusion | flops 4194304 | bytes 25165824 | tf_op jit(solution)/shard_map/mul | solution.py:79
  180.9 13.6 %collective-permute-done.2 = bf16[128,4096]{1,0:T(8,128)(2,1)} collective-permute-done((bf16[128,4096]{1,0:T(8,128)(2,1)}, bf16[128,4096]{1,0:T(8,128)(2,1)}, u32[]{:S(2)}, u32[]{:S(2)}) %collective-permute-start.2) | collective-permute-done | bytes 1048608 | tf_op jit(solution)/shard_map/ppermute | solution.py:128
  194.5 23.3 %collective-permute-done.1 = bf16[128,4096]{1,0:T(8,128)(2,1)S(1)} collective-permute-done((bf16[128,4096]{1,0:T(8,128)(2,1)}, bf16[128,4096]{1,0:T(8,128)(2,1)S(1)}, u32[]{:S(2)}, u32[]{:S(2)}) %collective-permute-start.1) | collective-permute-done | bytes 1048608 | tf_op jit(solution)/shard_map/ppermute | solution.py:126
  236.0 7.0 multiply_reduce_fusion
  247.8 10.3 %convolution_convert_fusion.2 = bf16[512,4096]{1,0:T(8,128)(2,1)} fusion(bf16[512,1024]{0,1:T(8,128)(2,1)} %bitcast.161, bf16[1024,4096]{1,0:T(8,128)(2,1)} %bitcast_multiply_fusion.1), kind=kOutput, calls=%fused_computation.11 | convolution fusion | flops 4297064448 | bytes 13631488 | tf_op jit(solution)/shard_map/dot_general | solution.py:107
  258.3 8.8 %mul.111.clone = bf16[32,128,3,8,128]{1,0,4,3,2:T(8,128)(2,1)} broadcast(bf16[32,3,8]{0,2,1:T(8,128)(2,1)S(1)} %convert_bitcast_fusion.3), dimensions={0,2,3} | broadcast | bytes 25167360 | tf_op jit(solution)/shard_map/mul | solution.py:76
  267.1 37.6 %mul.132 = bf16[4096,3,1024]{0,2,1:T(8,128)(2,1)} reshape(bf16[32,128,3,8,128]{1,0,4,3,2:T(8,128)(2,1)} %mul.111.clone) | data formatting | bytes 50331648 | tf_op jit(solution)/shard_map/mul | solution.py:76
  304.8 28.8 %mul.133 = bf16[4096,3,1024]{0,2,1:T(8,128)(2,1)} multiply(bf16[4096,3,1024]{0,2,1:T(8,128)(2,1)} %copy.50, bf16[4096,3,1024]{0,2,1:T(8,128)(2,1)} %mul.132) | non-fusion elementwise | flops 12582912 | bytes 75497472 | tf_op jit(solution)/shard_map/mul | solution.py:76
  345.7 8.1 %while.23 = (s32[]{:T(128)}, f32[8,128,128]{2,1,0:T(8,128)S(1)}, s32[]{:T(128)}, bf16[8,8,128,128]{3,2,1,0:T(8,128)(2,1)}, s32[]{:T(128)}, /*index=5*/s32[]{:T(128)}, s32[]{:T(128)}, s32[]{:T(128)}) while((s32[]{:T(128)}, f32[8,128,128]{2,1,0:T(8,128)S(1)}, s32[]{:T(128)}, bf16[8,8,128,128]{3,2,1,0:T(8,128)(2,1)}, s32[]{:T(128)}, ...), condition=%wide.region_6.7_spmd, body=%wide.region_5.6_spmd.sunk | while | flops 262150 | bytes 1310863 | solution.py:43
  359.7 19.6 %convolution_convert_fusion.1 = bf16[512,4096]{1,0:T(8,128)(2,1)} fusion(bf16[512,3072]{0,1:T(8,128)(2,1)S(1)} %bitcast.158, bf16[4096,3072]{0,1:T(8,128)(2,1)} %bitcast.142), kind=kOutput, calls=%fused_computation.10 | convolution fusion | flops 12886999040 | bytes 32505856 | tf_op jit(solution)/shard_map/tc,mc->tm/dot_general | solution.py:191
  379.6 10.3 %convolution_convert_fusion = bf16[4096,1024]{1,0:T(8,128)(2,1)} fusion(bf16[512,4096]{1,0:T(8,128)(2,1)} %bitcast.155, bf16[512,1024]{0,1:T(8,128)(2,1)} %bitcast.162), kind=kOutput, calls=%fused_computation.8 | convolution fusion | flops 4299161600 | bytes 13631488 | tf_op jit(solution)/shard_map/tm,tf->mf/dot_general | solution.py:139
  390.0 19.0 %convert_bitcast_fusion = bf16[4096,3072]{0,1:T(8,128)(2,1)} fusion(bf16[512,3072]{0,1:T(8,128)(2,1)S(1)} %bitcast.159, bf16[512,4096]{1,0:T(8,128)(2,1)} %all-gather.6.cloned.1.call-done), kind=kOutput, calls=%fused_computation.4 | convolution fusion | flops 12897484800 | bytes 32505856 | tf_op jit(solution)/shard_map/tm,tc->mc/dot_general | solution.py:180
  413.1 7.2 %reshape.127 = f32[512,3,1024]{2,0,1:T(8,128)} reshape(f32[4,128,3,8,128]{4,3,1,0,2:T(8,128)} %broadcast_in_dim.21) | data formatting | bytes 12582912 | tf_op jit(solution)/shard_map/reshape | solution.py:188
  423.0 32.6 %reduce-scatter.7.cloned.1.call-done = bf16[128,4096]{1,0:T(8,128)(2,1)} async-done(((bf16[512,4096]{1,0:T(8,128)(2,1)}), bf16[128,4096]{1,0:T(8,128)(2,1)}) %reduce-scatter.7.cloned.1.call-update) | async-done | bytes 1048592 | tf_op jit(solution)/shard_map/reduce_scatter | solution.py:190
  458.0 72.7 %reduce-scatter.11.cloned.1.call-done = bf16[512,1024]{1,0:T(8,128)(2,1)} async-done(((bf16[4096,1024]{1,0:T(8,128)(2,1)}), bf16[512,1024]{1,0:T(8,128)(2,1)}) %reduce-scatter.11.cloned.1.call-update) | async-done | bytes 1048592 | tf_op jit(solution)/shard_map/reduce_scatter | solution.py:140
  534.6 157.0 %reduce-scatter.9.cloned.1.call-done = bf16[512,3072]{0,1:T(8,128)(2,1)} async-done(((bf16[4096,3072]{0,1:T(8,128)(2,1)}), bf16[512,3072]{0,1:T(8,128)(2,1)}) %reduce-scatter.9.cloned.1.call-update) | async-done | bytes 3145744 | tf_op jit(solution)/shard_map/reduce_scatter | solution.py:181
  691.6 5.4 copy.68
  697.0 9.5 %multiply_multiply_fusion = f32[512,3,1024]{2,0,1:T(8,128)} fusion(f32[512,3,1024]{2,0,1:T(8,128)} %copy.68, f32[512,3,1024]{2,0,1:T(8,128)} %reshape.127), kind=kLoop, calls=%fused_computation.9 | loop fusion | flops 3145728 | bytes 18874368 | tf_op jit(solution)/shard_map/mul | solution.py:189
  (99 shorter events, 71.8 us)
Async XLA Ops:
  7.2 141.5 %all-gather.6.cloned.1.call-start = ((), (), s32[]{:S(2)}) async-start(), calls=%async_computation.4 | async-start | bytes 5242880 | tf_op jit(solution)/shard_map/all_gather | solution.py:82
  7.9 224.6 %all-gather.8.cloned.1.call-start = ((), (), s32[]{:S(2)}) async-start(), calls=%async_computation.9 | async-start | bytes 2359296 | tf_op jit(solution)/shard_map/all_gather | solution.py:21
  7.9 162.8 %collective-permute-start = (bf16[128,4096]{1,0:T(8,128)(2,1)}, bf16[128,4096]{1,0:T(8,128)(2,1)}, u32[]{:S(2)}, u32[]{:S(2)}) collective-permute-start(bf16[128,4096]{1,0:T(8,128)(2,1)} %param.19), channel_id=1, source_target_pairs={{0,1},{1,2},{2,3},{3,0},{4,5},{5,6},{6,7},{7,4},{8,9},{9,10},{10,1... | collective-permute-start | bytes 3145736 | tf_op jit(solution)/shard_map/ppermute | solution.py:126
  89.6 33.6 %copy-start.11 = (s32[512,8]{0,1:T(8,128)S(1)}, s32[512,8]{0,1:T(8,128)}, u32[]{:S(2)}) copy-start(s32[512,8]{0,1:T(8,128)} %param.13) | copy-start | bytes 49156
  89.6 33.6 %copy-start.12 = (s32[512,8]{0,1:T(8,128)S(1)}, s32[512,8]{0,1:T(8,128)}, u32[]{:S(2)}) copy-start(s32[512,8]{0,1:T(8,128)} %param.14) | copy-start | bytes 49156
  166.9 60.8 %copy-start = (bf16[3072,512]{1,0:T(8,128)(2,1)}, bf16[3072,512]{1,0:T(8,128)(2,1)S(1)}, u32[]{:S(2)}) copy-start(bf16[3072,512]{1,0:T(8,128)(2,1)S(1)} %convolution_convert_fusion.3) | copy-start | bytes 9437188
  166.9 3.8 copy-start.13
  168.4 177.3 %all-gather.10.cloned.1.call-start = ((), (), s32[]{:S(2)}) async-start(), calls=%async_computation.10 | async-start | bytes 2359296 | tf_op jit(solution)/shard_map/all_gather | solution.py:34
  168.5 26.1 %collective-permute-start.2 = (bf16[128,4096]{1,0:T(8,128)(2,1)}, bf16[128,4096]{1,0:T(8,128)(2,1)}, u32[]{:S(2)}, u32[]{:S(2)}) collective-permute-start(bf16[128,4096]{1,0:T(8,128)(2,1)} %param.19), channel_id=1, source_target_pairs={{1,0},{2,1},{3,2},{0,3},{5,4},{6,5},{7,6},{4,7},{9,8},{10,9},{11,1... | collective-permute-start | bytes 3145736 | tf_op jit(solution)/shard_map/ppermute | solution.py:128
  170.8 47.0 %collective-permute-start.1 = (bf16[128,4096]{1,0:T(8,128)(2,1)}, bf16[128,4096]{1,0:T(8,128)(2,1)S(1)}, u32[]{:S(2)}, u32[]{:S(2)}) collective-permute-start(bf16[128,4096]{1,0:T(8,128)(2,1)} %collective-permute-done), channel_id=1, source_target_pairs={{0,1},{1,2},{2,3},{3,0},{4,5},{5,6},{6,7},{7,4},{8,9},{9,10},{10,1... | collective-permute-start | bytes 3145736 | tf_op jit(solution)/shard_map/ppermute | solution.py:126
  172.0 45.8 %copy-start.7 = (bf16[128,4096]{1,0:T(8,128)(2,1)S(1)}, bf16[128,4096]{1,0:T(8,128)(2,1)}, u32[]{:S(2)}) copy-start(bf16[128,4096]{1,0:T(8,128)(2,1)} %param.19) | copy-start | bytes 3145732
  227.7 2.0 copy-start.2
  232.7 3.3 copy-start.6
  247.8 172.7 %reduce-scatter.5.cloned.1.call-start = ((), (), s32[]{:S(2)}) async-start(), calls=%async_computation.5 | async-start | bytes 5242880 | tf_op jit(solution)/shard_map/reduce_scatter | solution.py:106
  258.1 197.5 %reduce-scatter.7.cloned.1.call-start = ((), (), s32[]{:S(2)}) async-start(), calls=%async_computation.6 | async-start | bytes 5242880 | tf_op jit(solution)/shard_map/reduce_scatter | solution.py:190
  333.6 2.7 copy-start.1
  340.7 2.9 copy-start.3
  353.8 3.2 copy-start.4
  356.9 2.5 copy-start.9
  379.3 151.3 %reduce-scatter.11.cloned.1.call-start = ((), (), s32[]{:S(2)}) async-start(), calls=%async_computation.8 | async-start | bytes 9437184 | tf_op jit(solution)/shard_map/reduce_scatter | solution.py:140
  389.9 301.7 %reduce-scatter.9.cloned.1.call-start = ((), (), s32[]{:S(2)}) async-start(), calls=%async_computation.7 | async-start | bytes 28311552 | tf_op jit(solution)/shard_map/reduce_scatter | solution.py:181
  413.1 7.2 %copy-start.14 = (s32[8,32]{1,0:T(8,128)S(1)}, s32[8,32]{1,0:T(8,128)}, u32[]{:S(2)}) copy-start(s32[8,32]{1,0:T(8,128)} %param.18) | copy-start | bytes 3076
  413.1 7.4 %copy-start.5 = (bf16[128,4096]{1,0:T(8,128)(2,1)S(1)}, bf16[128,4096]{1,0:T(8,128)(2,1)}, u32[]{:S(2)}) copy-start(bf16[128,4096]{1,0:T(8,128)(2,1)} %param.12) | copy-start | bytes 3145732
  420.3 35.3 %copy-start.8 = (bf16[128,4096]{1,0:T(8,128)(2,1)S(1)}, bf16[128,4096]{1,0:T(8,128)(2,1)}, u32[]{:S(2)}) copy-start(bf16[128,4096]{1,0:T(8,128)(2,1)} %param.19) | copy-start | bytes 3145732
  (1 other events, 0.7 us)
Sparse Core Ops, SparseCore 0:
  9.6 95.0 all-gather.5
  168.5 27.9 all-gather.7
  247.9 34.4 all-gather.9
  284.5 76.7 reduce-scatter.4
  379.5 76.0 reduce-scatter.6
  458.9 71.7 reduce-scatter.10
  534.7 156.8 reduce-scatter.8
